TPU v7x, 512 devices: a whole 4x4x16 slice. The times are simulated.
512 devices in a mesh: template: 16 (over y, x_hi, core), fsdp: 16 (over z), dp: 2 (over x_lo).
Axes of the slice: x: 4 (x_hi: 2, x_lo: 2; x = x_hi * 2 + x_lo), y: 4, z: 16, core: 2. Of those that a mesh axis runs over, the one named last changes fastest.
Arguments:
- hidden: bfloat16 [16, 4096, 8192], P('template', ('fsdp', 'dp')), may hold values from -6 to 6
- target: bfloat16 [16, 4096, 512], P('template', ('fsdp', 'dp')), may hold values from -6 to 6
- weight: bfloat16 [16, 8192, 512], P('template', 'fsdp'), may hold values from -6 to 6
- gain: bfloat16 [16, 8192], P('template', 'fsdp'), may hold values from 0.099609375 to 1.8984375
Outputs:
- merged_weight: float32 [8192, 512], P(('fsdp', 'dp'))
- merged_gain: float32 [8192], P(('fsdp', 'dp'))
All inputs are finite; a program needn't handle non-finite values.
Results may differ from a plain program's by a relative error of at most 0.0018.
Values may be sent and summed in bfloat16 or wider, within the bound.
No kernel may reach another device: no remote copies, remote signals or barrier semaphores. Data moves between devices by JAX's collectives and lax.ppermute only.
A program may use at most 64 MiB of HBM per device.

v0:
```python
import math
import jax
import jax.numpy as jnp
from jax import lax
from jax.sharding import PartitionSpec as P


def body(hidden, target, weight, gain):
    token_batch = hidden[0]
    goal = target[0]
    w_shard = weight[0]
    g_shard = gain[0]
    width = token_batch.shape[1]
    rows = w_shard.shape[0]
    heads = w_shard.shape[1]
    scale = 1.0 / math.sqrt(width)
    n_t = lax.axis_size("template")
    n_dp = lax.axis_size("dp")
    hidden_f = token_batch.astype(jnp.float32)
    ratio = lax.rsqrt(jnp.mean(jnp.square(hidden_f), axis=1, keepdims=True) + 1e-05)
    swap = [(i, (i + 1) % n_dp) for i in range(n_dp)]
    other_hidden = lax.ppermute(token_batch, "dp", swap)
    other_f = other_hidden.astype(jnp.float32)
    other_ratio = lax.rsqrt(jnp.mean(jnp.square(other_f), axis=1, keepdims=True) + 1e-05)
    half = heads // n_dp
    dp_at = lax.axis_index("dp")
    w_cols = lax.dynamic_slice_in_dim(w_shard, dp_at * half, half, 1)
    w_ext = jnp.concatenate([w_cols, g_shard.reshape(-1, half)], axis=0)
    gathered = lax.all_gather(w_ext, "fsdp", axis=0, tiled=False)
    w_half = gathered[:, :rows, :]
    g_full = gathered[:, rows:, :].reshape(-1).astype(jnp.float32)
    xhat = hidden_f * ratio
    normed = (xhat * g_full[None, :]).astype(jnp.bfloat16)
    other_normed = (other_f * other_ratio * g_full[None, :]).astype(jnp.bfloat16)
    n_blocks = gathered.shape[0]
    mine_half = jnp.einsum(
        "tfr,frh->th",
        normed.reshape(-1, n_blocks, rows),
        w_half,
        preferred_element_type=jnp.float32,
    )
    theirs_half = jnp.einsum(
        "tfr,frh->th",
        other_normed.reshape(-1, n_blocks, rows),
        w_half,
        preferred_element_type=jnp.float32,
    )
    from_other = lax.ppermute(theirs_half, "dp", swap)
    both = jnp.stack([mine_half, from_other])
    first = jnp.where(dp_at == 0, both[0], both[1])
    second = jnp.where(dp_at == 0, both[1], both[0])
    values = jnp.concatenate([first, second], axis=1) * scale
    delta = (values - goal.astype(jnp.float32)).astype(jnp.bfloat16)
    n_f = lax.axis_size("fsdp")
    by_dest = jnp.transpose(token_batch.reshape(token_batch.shape[0], n_f, rows), (1, 0, 2))
    late_batch, _ = lax.optimization_barrier((by_dest, theirs_half))
    local_hidden = lax.all_to_all(late_batch, "fsdp", 0, 0, tiled=True).reshape(-1, rows)
    local_ratio = lax.all_gather(ratio, "fsdp", axis=0, tiled=True)
    local_delta = lax.all_gather(delta, "fsdp", axis=0, tiled=True)
    local_xhat = local_hidden.astype(jnp.float32) * local_ratio
    g_f = g_shard.astype(jnp.float32)
    local_normed = (local_xhat * g_f[None, :]).astype(jnp.bfloat16)
    sq_normed = jnp.square(local_normed.astype(jnp.float32)).astype(jnp.bfloat16)
    sq_delta = jnp.square(local_delta.astype(jnp.float32)).astype(jnp.bfloat16)
    fisher = jnp.einsum("td,th->dh", sq_normed, sq_delta, preferred_element_type=jnp.float32)
    back = jnp.einsum("th,dh->td", local_delta, w_shard, preferred_element_type=jnp.float32) * scale
    gain_info = jnp.sum(jnp.square(back * local_xhat), axis=0)
    extra = jnp.zeros((rows, 128), jnp.float32)
    extra = extra.at[:, 0].set(gain_info * g_f).at[:, 1].set(gain_info)
    pack = jnp.concatenate([fisher * w_shard.astype(jnp.float32), fisher, extra], axis=1)
    cols = pack.shape[1]
    piece = rows // (n_t * n_dp)
    pack = pack.reshape(n_t * n_dp, piece, cols)
    parts = lax.all_to_all(pack, ("dp", "template"), 0, 0, tiled=True)
    total = jnp.sum(parts, axis=0)
    ratio_block = (
        jnp.zeros((piece, 128), jnp.float32)
        .at[:, 0]
        .set(total[:, 2 * heads] / total[:, 2 * heads + 1])
    )
    done = jnp.concatenate([total[:, :heads] / total[:, heads : 2 * heads], ratio_block], axis=1)
    spread = lax.all_to_all(
        jnp.broadcast_to(done[None], (n_t,) + done.shape), "template", 0, 0, tiled=True
    )
    full = spread.reshape(n_t * piece, done.shape[1])
    merged = full[:, :heads]
    merged_gain = full[:, heads]
    return (merged, merged_gain)


def solution(mesh):
    in_specs = (
        P("template", ("fsdp", "dp"), None),
        P("template", ("fsdp", "dp"), None),
        P("template", "fsdp", None),
        P("template", "fsdp"),
    )
    out_specs = (P(("fsdp", "dp"), None), P(("fsdp", "dp")))
    return jax.shard_map(body, mesh=mesh, in_specs=in_specs, out_specs=out_specs, check_vma=False)
```

profile of v0, /device:TPU:1, one launch (start us, length us, event | category | flops | bytes accessed | tf_op | source)
XLA Modules:
  0.0 301.3 jit_solution(15434402891482876748)
XLA Ops:
  7.2 0.0 all-gather.9.cloned.1.call-start
  7.2 0.8 fusion.35
  8.0 1.0 dynamic-slice_bitcast_fusion
  9.0 0.7 maximum_bitcast_fusion
  9.7 0.0 all-gather.9.cloned.1.call-update
  9.7 4.0 %collective-permute-start = (bf16[128,8192]{1,0:T(8,128)(2,1)}, bf16[128,8192]{1,0:T(8,128)(2,1)S(1)}, u32[]{:S(2)}, u32[]{:S(2)}) collective-permute-start(bf16[128,8192]{1,0:T(8,128)(2,1)} %bitcast.50), channel_id=1, source_target_pairs={{0,1},{1,0},{2,3},{3,2},{4,5},{5,4},{6,7},{7,6},{8,9},{9,8},{10,11... | collective-permute-start | bytes 6291464 | tf_op jit(solution)/shard_map/ppermute | solution.py:22
  13.7 2.4 copy.21
  16.1 0.0 copy-start.1
  16.1 1.3 copy-done.1
  17.5 2.5 copy.37
  20.0 34.3 %collective-permute-done = bf16[128,8192]{1,0:T(8,128)(2,1)S(1)} collective-permute-done((bf16[128,8192]{1,0:T(8,128)(2,1)}, bf16[128,8192]{1,0:T(8,128)(2,1)S(1)}, u32[]{:S(2)}, u32[]{:S(2)}) %collective-permute-start) | collective-permute-done | bytes 2097184 | tf_op jit(solution)/shard_map/ppermute | solution.py:22
  54.3 0.5 fusion
  54.8 31.8 %all-gather.9.cloned.1.call-done = bf16[16,514,256]{2,1,0:T(8,128)(2,1)} async-done(((bf16[1,514,256]{2,1,0:T(8,128)(2,1)}), bf16[16,514,256]{2,1,0:T(8,128)(2,1)}) %all-gather.9.cloned.1.call-update) | async-done | bytes 4210704 | tf_op jit(solution)/shard_map/all_gather | solution.py:29
  86.7 1.0 slice_convert_fusion
  87.7 0.6 fusion.2
  88.3 0.6 copy-done.5
  88.9 0.7 fusion.24
  89.6 0.0 copy-start
  89.6 6.2 %all-to-all-start = ((bf16[16,128,512]{2,1,0:T(8,128)(2,1)}), bf16[16,128,512]{2,1,0:T(8,128)(2,1)}, u32[]{:S(2)}, u32[]{:S(2)}) async-start(bf16[16,128,512]{2,1,0:T(8,128)(2,1)} %bitcast.52), calls=%async_computation | async-start | bytes 4194304 | tf_op jit(solution)/shard_map/all_to_all | solution.py:57
  95.9 0.0 all-gather.7.cloned.1.call-start
  95.9 0.5 multiply_reduce_fusion
  96.4 3.1 %collective-permute-start.1 = (f32[128,256]{1,0:T(8,128)S(1)}, f32[128,256]{1,0:T(8,128)S(1)}, u32[]{:S(2)}, u32[]{:S(2)}) collective-permute-start(f32[128,256]{1,0:T(8,128)S(1)} %fusion.24), channel_id=1, source_target_pairs={{0,1},{1,0},{2,3},{3,2},{4,5},{5,4},{6,7},{7,6},{8,9},{9,8},{10,11... | collective-permute-start | bytes 393224 | tf_op jit(solution)/shard_map/ppermute | solution.py:48
  99.6 0.0 copy-start.3
  99.6 0.0 copy-start.2
  99.6 5.5 %fusion.21 = f32[128,256]{1,0:T(8,128)S(1)} fusion(bf16[16,514,256]{2,1,0:T(8,128)(2,1)} %all-gather.9.cloned.1.call-done, f32[16,512]{1,0:T(8,128)S(1)} %bitcast.60, f32[128]{0:T(128)S(1)} %get-tuple-element.49, bf16[128,16,512]{2,1,0:T(8,128)(2,1)} %bitcast.54), kind=kOutput, calls=%fused_computation.29 | convolution fusion | flops 541065216 | bytes 6455808 | tf_op jit(solution)/shard_map/tfr,frh->th/dot_general | solution.py:36
  105.1 0.0 collective-permute-done.1
  105.1 0.0 copy-done.3
  105.1 0.7 fusion.31
  105.8 0.0 all-gather.7.cloned.1.call-update
  105.8 0.2 copy.18
  106.1 0.6 compare_reduce_fusion.1
  106.7 0.6 compare_reduce_fusion
  107.3 111.4 %all-gather.3 = f32[16,1,128]{2,1,0:T(1,128)S(1)} all-gather(f32[1,1,128]{2,1,0:T(1,128)S(1)} %get-tuple-element.48), channel_id=3, replica_groups=mesh['template'=16,'fsdp'=16,'dp'=2] {'fsdp'}, dimensions={0}, use_global_device_ids=true | all-gather | bytes 8704 | tf_op jit(solution)/shard_map/all_gather | solution.py:58
  218.7 2.2 all-gather.7.cloned.1.call-done
  220.9 0.0 all-to-all-done
  220.9 4.0 %fusion.7 = f32[512]{0:T(512)S(1)} fusion(bf16[2048,512]{1,0:T(8,128)(2,1)} %bitcast.16, bf16[2048,512]{1,0:T(8,128)(2,1)} %all-gather.7.cloned.1.call-done, f32[2048]{0:T(1024)S(1)} %bitcast.61, bf16[1,512,512]{2,1,0:T(8,128)(2,1)S(1)} %copy-done.2), kind=kOutput, calls=%fused_computation.10 | convolution fusion | flops 1080032768 | bytes 4728832 | tf_op jit(solution)/shard_map/th,dh->td/dot_general | solution.py:66
  224.9 0.0 copy-done.4
  224.9 1.2 broadcast_select_fusion.2
  226.1 0.2 scatter.11
  226.4 3.3 %convert_multiply_fusion.3 = (f32[512,512]{0,1:T(8,128)S(1)}, f32[512,512]{0,1:T(8,128)S(1)}) fusion(bf16[1,512,512]{1,2,0:T(8,128)(2,1)S(1)} %copy.18, bf16[2048,512]{1,0:T(8,128)(2,1)S(1)} %copy-done.6, bf16[2048,512]{1,0:T(8,128)(2,1)} %bitcast.16, f32[2048]{0:T(1024)S(1)} %bitcast.62, f32[512]{0:T(512)S(1)} %bitcast.63), kind=kOutput, calls=%fused_computation.31 | convolution fusion | flops 1084751872 | bytes 6825984 | tf_op jit(solution)/shard_map/td,th->dh/dot_general | solution.py:65
  229.7 0.2 pad_maximum_fusion
  229.9 2.0 copy.19
  231.9 43.6 %all_to_all.15 = f32[32,16,1152]{2,1,0:T(8,128)S(1)} all-to-all(f32[32,16,1152]{2,1,0:T(8,128)} %bitcast.49), channel_id=1, replica_groups=mesh['template'=16,'fsdp'=16,'dp'=2] {'dp','template'}, dimensions={0} | all-to-all | bytes 4718592 | tf_op jit(solution)/shard_map/all_to_all | solution.py:74
  275.5 0.1 reduce_sum.42
  275.6 0.6 fusion.32
  276.3 16.6 %all_to_all.16 = f32[16,16,640]{2,1,0:T(8,128)S(1)} all-to-all(f32[16,16,640]{2,1,0:T(8,128)S(1)} %broadcast_in_dim.2), channel_id=1, replica_groups=mesh['template'=16,'fsdp'=16,'dp'=2] {'template'}, dimensions={0} | all-to-all | bytes 1310720 | tf_op jit(solution)/shard_map/all_to_all | solution.py:82
  293.0 0.9 slice.81
  293.8 0.7 slice_reduce_fusion
  (16 shorter events, 0.2 us)
Async XLA Ops:
  7.2 79.5 %all-gather.9.cloned.1.call-start = ((), (), s32[]{:S(2)}) async-start(), calls=%async_computation.4 | async-start | bytes 4526080 | tf_op jit(solution)/shard_map/all_gather | solution.py:29
  9.7 44.6 %collective-permute-start = (bf16[128,8192]{1,0:T(8,128)(2,1)}, bf16[128,8192]{1,0:T(8,128)(2,1)S(1)}, u32[]{:S(2)}, u32[]{:S(2)}) collective-permute-start(bf16[128,8192]{1,0:T(8,128)(2,1)} %bitcast.50), channel_id=1, source_target_pairs={{0,1},{1,0},{2,3},{3,2},{4,5},{5,4},{6,7},{7,6},{8,9},{9,8},{10,11... | collective-permute-start | bytes 6291464 | tf_op jit(solution)/shard_map/ppermute | solution.py:22
  16.1 1.4 copy-start.1
  86.7 2.2 copy-start.5
  89.6 6.3 %copy-start = (bf16[1,128,8192]{2,1,0:T(8,128)(2,1)S(1)}, bf16[1,128,8192]{2,1,0:T(8,128)(2,1)}, u32[]{:S(2)}) copy-start(bf16[1,128,8192]{2,1,0:T(8,128)(2,1)} %param.10) | copy-start | bytes 6291460
  89.6 131.3 %all-to-all-start = ((bf16[16,128,512]{2,1,0:T(8,128)(2,1)}), bf16[16,128,512]{2,1,0:T(8,128)(2,1)}, u32[]{:S(2)}, u32[]{:S(2)}) async-start(bf16[16,128,512]{2,1,0:T(8,128)(2,1)} %bitcast.52), calls=%async_computation | async-start | bytes 4194304 | tf_op jit(solution)/shard_map/all_to_all | solution.py:57
  95.9 125.0 %all-gather.7.cloned.1.call-start = ((), (), s32[]{:S(2)}) async-start(), calls=%async_computation.3 | async-start | bytes 2228224 | tf_op jit(solution)/shard_map/all_gather | solution.py:59
  96.4 8.6 %collective-permute-start.1 = (f32[128,256]{1,0:T(8,128)S(1)}, f32[128,256]{1,0:T(8,128)S(1)}, u32[]{:S(2)}, u32[]{:S(2)}) collective-permute-start(f32[128,256]{1,0:T(8,128)S(1)} %fusion.24), channel_id=1, source_target_pairs={{0,1},{1,0},{2,3},{3,2},{4,5},{5,4},{6,7},{7,6},{8,9},{9,8},{10,11... | collective-permute-start | bytes 393224 | tf_op jit(solution)/shard_map/ppermute | solution.py:48
  99.6 5.6 %copy-start.3 = (bf16[1,128,512]{2,1,0:T(8,128)(2,1)S(1)}, bf16[1,128,512]{2,1,0:T(8,128)(2,1)}, u32[]{:S(2)}) copy-start(bf16[1,128,512]{2,1,0:T(8,128)(2,1)} %param.11) | copy-start | bytes 393220
  99.6 6.3 %copy-start.2 = (bf16[1,512,512]{2,1,0:T(8,128)(2,1)S(1)}, bf16[1,512,512]{2,1,0:T(8,128)(2,1)}, u32[]{:S(2)}) copy-start(bf16[1,512,512]{2,1,0:T(8,128)(2,1)} %param.12) | copy-start | bytes 1572868
  220.9 4.0 %copy-start.4 = (bf16[1,512]{1,0:T(2,128)(2,1)S(1)}, bf16[1,512]{1,0:T(2,128)(2,1)}, u32[]{:S(2)}) copy-start(bf16[1,512]{1,0:T(2,128)(2,1)} %param.13) | copy-start | bytes 3076
  220.9 5.5 %copy-start.6 = (bf16[2048,512]{1,0:T(8,128)(2,1)S(1)}, bf16[2048,512]{1,0:T(8,128)(2,1)}, u32[]{:S(2)}) copy-start(bf16[2048,512]{1,0:T(8,128)(2,1)} %all-gather.7.cloned.1.call-done) | copy-start | bytes 6291460
Sparse Core Ops, SparseCore 0:
  10.7 75.9 all-gather.8
  106.0 114.8 all-gather.6
where the time goes:
time: 302 us; the launch traced here: 301 us
  blocking collectives  172 us (57%)
  waiting for transfers between devices  68.4 us (23%)
  between operations  14.3 us (5%)
  matrix products  13.4 us (4%)
  starting transfers between devices  13.3 us (4%)
  local copies, waits for them, and re-layouts  12 us (4%)
  other arithmetic  8.25 us (3%)
    all_gather x1, blocking collectives, body(): local_ratio = lax.all_gather(ratio, 'fsdp', axis=0, tiled=True)  111 us
    all_to_all x1, blocking collectives, body(): parts = lax.all_to_all(pack, ('dp', 'template'), 0, 0, tiled=True)  43.6 us
    ppermute x1, waiting for transfers between devices, body(): other_hidden = lax.ppermute(token_batch, 'dp', swap)  34.3 us
    all_gather x1, waiting for transfers between devices, body(): gathered = lax.all_gather(w_ext, 'fsdp', axis=0, tiled=False)  31.8 us
    all_to_all x1, blocking collectives, body(): lax.all_to_all(jnp.broadcast_to(done[None], (n_t,) + done.shape), 'templa...  16.6 us
    all_to_all x1, starting transfers between devices, body(): lax.all_to_all(late_batch, 'fsdp', 0, 0, tiled=True).reshape(-1, rows)  6.22 us
  transfers between devices with their start and end apart: 5, of which 3 were waited for; matrix products, arithmetic and copies ran while one was open for 5% of the time, Pallas kernels for 0%

commit v1 on v0

--- a/solution.py
+++ b/solution.py
@@ -6,6 +6,29 @@
 
 
 def body(hidden, target, weight, gain):
+
+    def state_pairs_all(vals):
+        k_now = jax.lax.axis_size("fsdp")
+        moved = jax.lax.axis_index("fsdp")
+        local_next, step_out, main = (k_now, moved, vals.shape[0])
+        log = [(k, (k + 1) % local_next) for k in range(local_next)]
+        pool = [(k, (k - 1) % local_next) for k in range(local_next)]
+        opened = jnp.zeros((*vals.shape[:0], local_next * main, *vals.shape[1:]), vals.dtype)
+        opened = lax.dynamic_update_slice_in_dim(opened, vals, step_out * main, axis=0)
+        arr_now = passed = vals
+        odd = local_next // 2
+        for j in range(1, odd + 1):
+            arr_now = jax.lax.ppermute(arr_now, "fsdp", log)
+            opened = lax.dynamic_update_slice_in_dim(
+                opened, arr_now, (step_out - j) % local_next * main, axis=0
+            )
+            if j < local_next - odd:
+                passed = jax.lax.ppermute(passed, "fsdp", pool)
+                opened = lax.dynamic_update_slice_in_dim(
+                    opened, passed, (step_out + j) % local_next * main, axis=0
+                )
+        return opened
+
     token_batch = hidden[0]
     goal = target[0]
     w_shard = weight[0]
@@ -55,7 +78,7 @@
     by_dest = jnp.transpose(token_batch.reshape(token_batch.shape[0], n_f, rows), (1, 0, 2))
     late_batch, _ = lax.optimization_barrier((by_dest, theirs_half))
     local_hidden = lax.all_to_all(late_batch, "fsdp", 0, 0, tiled=True).reshape(-1, rows)
-    local_ratio = lax.all_gather(ratio, "fsdp", axis=0, tiled=True)
+    local_ratio = state_pairs_all(ratio)
     local_delta = lax.all_gather(delta, "fsdp", axis=0, tiled=True)
     local_xhat = local_hidden.astype(jnp.float32) * local_ratio
     g_f = g_shard.astype(jnp.float32)

time: 302 us -> 330 us (1.093)
  blocking collectives: 172 us -> 69.5 us
  waiting for transfers between devices: 68.4 us -> 144 us
  starting transfers between devices: 13.3 us -> 64.8 us
    all_gather x1 -> x0, blocking collectives: 111 us -> none  [body(): local_ratio = lax.all_gather(ratio, 'fsdp', axis=0, tiled=True)]
    ppermute x0 -> x15, waiting for transfers between devices: none -> 78.2 us  [the longest x8 76.2 us: state_pairs_all(): arr_now = jax.lax.ppermute(arr_now, 'fsdp', log)]
    ppermute x0 -> x15, starting transfers between devices: none -> 51.4 us  [the longest x8 27.7 us: state_pairs_all(): arr_now = jax.lax.ppermute(arr_now, 'fsdp', log)]
    all_to_all x1, blocking collectives: 43.6 us -> 52.9 us  [body(): parts = lax.all_to_all(pack, ('dp', 'template'), 0, 0, tiled=True)]
  transfers between devices with their start and end apart: 5 -> 20, of which waited for: 3 -> 5; matrix products, arithmetic and copies ran while one was open for 5% -> 5% of each run, Pallas kernels for 0% -> 0%
where the time goes in v1:
time: 330 us; the launch traced here: 329 us
  waiting for transfers between devices  144 us (44%)
  blocking collectives  69.5 us (21%)
  starting transfers between devices  64.8 us (20%)
  between operations  14.8 us (4%)
  local copies, waits for them, and re-layouts  13.4 us (4%)
  matrix products  13.4 us (4%)
  other arithmetic  8.78 us (3%)
    ppermute x8, waiting for transfers between devices, state_pairs_all(): arr_now = jax.lax.ppermute(arr_now, 'fsdp', log)  76.2 us
    all_to_all x1, blocking collectives, body(): parts = lax.all_to_all(pack, ('dp', 'template'), 0, 0, tiled=True)  52.9 us
    ppermute x1, waiting for transfers between devices, body(): other_hidden = lax.ppermute(token_batch, 'dp', swap)  34.3 us
    all_gather x1, waiting for transfers between devices, body(): gathered = lax.all_gather(w_ext, 'fsdp', axis=0, tiled=False)  31.8 us
    ppermute x8, starting transfers between devices, state_pairs_all(): arr_now = jax.lax.ppermute(arr_now, 'fsdp', log)  27.7 us
    ppermute x7, starting transfers between devices, state_pairs_all(): passed = jax.lax.ppermute(passed, 'fsdp', pool)  23.7 us
    all_to_all x1, blocking collectives, body(): lax.all_to_all(jnp.broadcast_to(done[None], (n_t,) + done.shape), 'templa...  16.6 us
  transfers between devices with their start and end apart: 20, of which 5 were waited for; matrix products, arithmetic and copies ran while one was open for 5% of the time, Pallas kernels for 0%

profile of v1, /device:TPU:1, one launch (start us, length us, event | category | flops | bytes accessed | tf_op | source)
XLA Modules:
  0.0 329.2 jit_solution(7894327605468258051)
XLA Ops:
  7.2 0.8 fusion.36
  8.0 1.0 dynamic-slice_bitcast_fusion
  9.0 0.7 maximum_bitcast_fusion
  9.7 4.0 %collective-permute-start = (bf16[128,8192]{1,0:T(8,128)(2,1)}, bf16[128,8192]{1,0:T(8,128)(2,1)S(1)}, u32[]{:S(2)}, u32[]{:S(2)}) collective-permute-start(bf16[128,8192]{1,0:T(8,128)(2,1)} %bitcast.79), channel_id=1, source_target_pairs={{0,1},{1,0},{2,3},{3,2},{4,5},{5,4},{6,7},{7,6},{8,9},{9,8},{10,11... | collective-permute-start | bytes 6291464 | tf_op jit(solution)/shard_map/ppermute | solution.py:45
  13.7 2.4 copy.21
  16.1 1.4 copy-done.1
  17.5 2.5 copy.37
  20.0 34.3 %collective-permute-done = bf16[128,8192]{1,0:T(8,128)(2,1)S(1)} collective-permute-done((bf16[128,8192]{1,0:T(8,128)(2,1)}, bf16[128,8192]{1,0:T(8,128)(2,1)S(1)}, u32[]{:S(2)}, u32[]{:S(2)}) %collective-permute-start) | collective-permute-done | bytes 2097184 | tf_op jit(solution)/shard_map/ppermute | solution.py:45
  54.3 0.5 fusion
  54.8 31.8 %all-gather.7.cloned.1.call-done = bf16[16,514,256]{2,1,0:T(8,128)(2,1)} async-done(((bf16[1,514,256]{2,1,0:T(8,128)(2,1)}), bf16[16,514,256]{2,1,0:T(8,128)(2,1)}) %all-gather.7.cloned.1.call-update) | async-done | bytes 4210704 | tf_op jit(solution)/shard_map/all_gather | solution.py:52
  86.7 1.0 slice_convert_fusion
  87.7 0.6 fusion.2
  88.4 0.5 copy-done.5
  88.9 0.7 fusion.24
  89.6 6.2 %all-to-all-start = ((bf16[16,128,512]{2,1,0:T(8,128)(2,1)}), bf16[16,128,512]{2,1,0:T(8,128)(2,1)}, u32[]{:S(2)}, u32[]{:S(2)}) async-start(bf16[16,128,512]{2,1,0:T(8,128)(2,1)} %bitcast.81), calls=%async_computation | async-start | bytes 4194304 | tf_op jit(solution)/shard_map/all_to_all | solution.py:80
  95.9 0.5 multiply_reduce_fusion
  96.6 3.1 collective-permute-start.16
  99.7 5.5 %fusion.21 = f32[128,256]{1,0:T(8,128)S(1)} fusion(bf16[16,514,256]{2,1,0:T(8,128)(2,1)} %all-gather.7.cloned.1.call-done, f32[16,512]{1,0:T(8,128)S(1)} %bitcast.89, f32[128]{0:T(128)S(1)} %get-tuple-element.50, bf16[128,16,512]{2,1,0:T(8,128)(2,1)} %bitcast.83), kind=kOutput, calls=%fused_computation.29 | convolution fusion | flops 541065216 | bytes 6455808 | tf_op jit(solution)/shard_map/tfr,frh->th/dot_general | solution.py:59
  105.2 0.7 fusion.31
  106.0 3.2 collective-permute-start.1
  109.2 3.3 collective-permute-start.2
  113.0 0.7 compare_reduce_fusion.1
  113.7 0.6 compare_reduce_fusion
  114.4 72.9 %collective-permute-done.1 = f32[128,1]{0,1:T(1,128)S(1)} collective-permute-done((f32[128,1]{0,1:T(1,128)S(1)}, f32[128,1]{0,1:T(1,128)S(1)}, u32[]{:S(2)}, u32[]{:S(2)}) %collective-permute-start.1) | collective-permute-done | bytes 544 | tf_op jit(solution)/shard_map/ppermute | solution.py:21
  187.2 8.4 %collective-permute-start.3 = (f32[128,1]{0,1:T(1,128)S(1)}, f32[128,1]{0,1:T(1,128)S(1)}, u32[]{:S(2)}, u32[]{:S(2)}) collective-permute-start(f32[128,1]{0,1:T(1,128)S(1)} %collective-permute-done.1), channel_id=1, source_target_pairs={{0,2},{2,4},{4,6},{6,8},{8,10},{10,12},{12,14},{14,16},{16,18},{18... | collective-permute-start | bytes 1544 | tf_op jit(solution)/shard_map/ppermute | solution.py:21
  195.7 1.9 collective-permute-done.2
  197.6 1.9 collective-permute-start.4
  199.7 4.9 %collective-permute-start.5 = (f32[128,1]{0,1:T(1,128)S(1)}, f32[128,1]{0,1:T(1,128)S(1)}, u32[]{:S(2)}, u32[]{:S(2)}) collective-permute-start(f32[128,1]{0,1:T(1,128)S(1)} %collective-permute-done.3), channel_id=1, source_target_pairs={{0,2},{2,4},{4,6},{6,8},{8,10},{10,12},{12,14},{14,16},{16,18},{18... | collective-permute-start | bytes 1544 | tf_op jit(solution)/shard_map/ppermute | solution.py:21
  204.6 1.9 collective-permute-start.6
  206.8 3.4 %collective-permute-start.7 = (f32[128,1]{0,1:T(1,128)S(1)}, f32[128,1]{0,1:T(1,128)S(1)}, u32[]{:S(2)}, u32[]{:S(2)}) collective-permute-start(f32[128,1]{0,1:T(1,128)S(1)} %collective-permute-done.5), channel_id=1, source_target_pairs={{0,2},{2,4},{4,6},{6,8},{8,10},{10,12},{12,14},{14,16},{16,18},{18... | collective-permute-start | bytes 1544 | tf_op jit(solution)/shard_map/ppermute | solution.py:21
  210.1 3.1 collective-permute-start.8
  213.5 2.1 collective-permute-start.9
  215.6 4.3 %collective-permute-start.10 = (f32[128,1]{0,1:T(1,128)S(1)}, f32[128,1]{0,1:T(1,128)S(1)}, u32[]{:S(2)}, u32[]{:S(2)}) collective-permute-start(f32[128,1]{0,1:T(1,128)S(1)} %collective-permute-done.8), channel_id=1, source_target_pairs={{0,30},{2,0},{4,2},{6,4},{8,6},{10,8},{12,10},{14,12},{16,14},{18,... | collective-permute-start | bytes 1544 | tf_op jit(solution)/shard_map/ppermute | solution.py:26
  220.2 1.9 collective-permute-start.11
  222.1 4.6 %collective-permute-start.12 = (f32[128,1]{0,1:T(1,128)S(1)}, f32[128,1]{0,1:T(1,128)S(1)}, u32[]{:S(2)}, u32[]{:S(2)}) collective-permute-start(f32[128,1]{0,1:T(1,128)S(1)} %collective-permute-done.10), channel_id=1, source_target_pairs={{0,30},{2,0},{4,2},{6,4},{8,6},{10,8},{12,10},{14,12},{16,14},{18,... | collective-permute-start | bytes 1544 | tf_op jit(solution)/shard_map/ppermute | solution.py:26
  226.9 1.9 collective-permute-start.13
  228.8 4.6 %collective-permute-start.14 = (f32[128,1]{0,1:T(1,128)S(1)}, f32[128,1]{0,1:T(1,128)S(1)}, u32[]{:S(2)}, u32[]{:S(2)}) collective-permute-start(f32[128,1]{0,1:T(1,128)S(1)} %collective-permute-done.12), channel_id=1, source_target_pairs={{0,30},{2,0},{4,2},{6,4},{8,6},{10,8},{12,10},{14,12},{16,14},{18,... | collective-permute-start | bytes 1544 | tf_op jit(solution)/shard_map/ppermute | solution.py:26
  233.6 1.9 collective-permute-start.15
  235.8 3.4 %collective-permute-done.15 = f32[128,1]{0,1:T(1,128)S(1)} collective-permute-done((f32[128,1]{0,1:T(1,128)S(1)}, f32[128,1]{0,1:T(1,128)S(1)}, u32[]{:S(2)}, u32[]{:S(2)}) %collective-permute-start.15) | collective-permute-done | bytes 544 | tf_op jit(solution)/shard_map/ppermute | solution.py:21
  239.4 4.0 %fusion.7 = f32[512]{0:T(512)S(1)} fusion(bf16[2048,512]{1,0:T(8,128)(2,1)} %bitcast.30, bf16[2048,512]{1,0:T(8,128)(2,1)} %all-gather.5.cloned.1.call-done, f32[2048]{0:T(1024)S(1)} %bitcast_dynamic-update-slice_fusion, bf16[1,512,512]{2,1,0:T(8,128)(2,1)S(1)} %copy-done.2), kind=kOutput, calls=%fused_computation.10 | convolution fusion | flops 1080032768 | bytes 4728832 | tf_op jit(solution)/shard_map/th,dh->td/dot_general | solution.py:89
  243.4 1.3 broadcast_select_fusion.2
  244.8 3.3 convert_multiply_fusion.3
  248.3 2.0 copy.19
  250.3 52.9 %all_to_all.15 = f32[32,16,1152]{2,1,0:T(8,128)S(1)} all-to-all(f32[32,16,1152]{2,1,0:T(8,128)} %bitcast.78), channel_id=1, replica_groups=mesh['template'=16,'fsdp'=16,'dp'=2] {'dp','template'}, dimensions={0} | all-to-all | bytes 4718592 | tf_op jit(solution)/shard_map/all_to_all | solution.py:97
  303.4 0.8 fusion.32
  304.2 16.6 %all_to_all.16 = f32[16,16,640]{2,1,0:T(8,128)S(1)} all-to-all(f32[16,16,640]{2,1,0:T(8,128)S(1)} %broadcast_in_dim.2), channel_id=1, replica_groups=mesh['template'=16,'fsdp'=16,'dp'=2] {'template'}, dimensions={0} | all-to-all | bytes 1310720 | tf_op jit(solution)/shard_map/all_to_all | solution.py:105
  320.8 0.9 slice.81
  321.7 0.7 slice_reduce_fusion
  (61 shorter events, 2.7 us)
Async XLA Ops:
  7.2 79.5 %all-gather.7.cloned.1.call-start = ((), (), s32[]{:S(2)}) async-start(), calls=%async_computation.4 | async-start | bytes 4526080 | tf_op jit(solution)/shard_map/all_gather | solution.py:52
  9.7 44.6 %collective-permute-start = (bf16[128,8192]{1,0:T(8,128)(2,1)}, bf16[128,8192]{1,0:T(8,128)(2,1)S(1)}, u32[]{:S(2)}, u32[]{:S(2)}) collective-permute-start(bf16[128,8192]{1,0:T(8,128)(2,1)} %bitcast.79), channel_id=1, source_target_pairs={{0,1},{1,0},{2,3},{3,2},{4,5},{5,4},{6,7},{7,6},{8,9},{9,8},{10,11... | collective-permute-start | bytes 6291464 | tf_op jit(solution)/shard_map/ppermute | solution.py:45
  16.1 1.4 copy-start.1
  86.7 2.2 copy-start.5
  89.6 6.3 %copy-start = (bf16[1,128,8192]{2,1,0:T(8,128)(2,1)S(1)}, bf16[1,128,8192]{2,1,0:T(8,128)(2,1)}, u32[]{:S(2)}) copy-start(bf16[1,128,8192]{2,1,0:T(8,128)(2,1)} %param.10) | copy-start | bytes 6291460
  89.6 149.7 %all-to-all-start = ((bf16[16,128,512]{2,1,0:T(8,128)(2,1)}), bf16[16,128,512]{2,1,0:T(8,128)(2,1)}, u32[]{:S(2)}, u32[]{:S(2)}) async-start(bf16[16,128,512]{2,1,0:T(8,128)(2,1)} %bitcast.81), calls=%async_computation | async-start | bytes 4194304 | tf_op jit(solution)/shard_map/all_to_all | solution.py:80
  95.9 143.5 %all-gather.5.cloned.1.call-start = ((), (), s32[]{:S(2)}) async-start(), calls=%async_computation.3 | async-start | bytes 2228224 | tf_op jit(solution)/shard_map/all_gather | solution.py:82
  96.6 8.6 %collective-permute-start.16 = (f32[128,256]{1,0:T(8,128)S(1)}, f32[128,256]{1,0:T(8,128)S(1)}, u32[]{:S(2)}, u32[]{:S(2)}) collective-permute-start(f32[128,256]{1,0:T(8,128)S(1)} %fusion.24), channel_id=1, source_target_pairs={{0,1},{1,0},{2,3},{3,2},{4,5},{5,4},{6,7},{7,6},{8,9},{9,8},{10,11... | collective-permute-start | bytes 393224 | tf_op jit(solution)/shard_map/ppermute | solution.py:71
  99.7 5.6 %copy-start.3 = (bf16[1,128,512]{2,1,0:T(8,128)(2,1)S(1)}, bf16[1,128,512]{2,1,0:T(8,128)(2,1)}, u32[]{:S(2)}) copy-start(bf16[1,128,512]{2,1,0:T(8,128)(2,1)} %param.11) | copy-start | bytes 393220
  99.7 13.0 %copy-start.2 = (bf16[1,512,512]{2,1,0:T(8,128)(2,1)S(1)}, bf16[1,512,512]{2,1,0:T(8,128)(2,1)}, u32[]{:S(2)}) copy-start(bf16[1,512,512]{2,1,0:T(8,128)(2,1)} %param.12) | copy-start | bytes 1572868
  106.0 81.3 %collective-permute-start.1 = (f32[128,1]{0,1:T(1,128)S(1)}, f32[128,1]{0,1:T(1,128)S(1)}, u32[]{:S(2)}, u32[]{:S(2)}) collective-permute-start(f32[128,1]{0,1:T(1,128)S(1)} %get-tuple-element.48), channel_id=1, source_target_pairs={{0,2},{2,4},{4,6},{6,8},{8,10},{10,12},{12,14},{14,16},{16,18},{18... | collective-permute-start | bytes 1544 | tf_op jit(solution)/shard_map/ppermute | solution.py:21
  109.2 88.4 %collective-permute-start.2 = (f32[128,1]{0,1:T(1,128)S(1)}, f32[128,1]{0,1:T(1,128)S(1)}, u32[]{:S(2)}, u32[]{:S(2)}) collective-permute-start(f32[128,1]{0,1:T(1,128)S(1)} %get-tuple-element.48), channel_id=1, source_target_pairs={{0,30},{2,0},{4,2},{6,4},{8,6},{10,8},{12,10},{14,12},{16,14},{18,... | collective-permute-start | bytes 1544 | tf_op jit(solution)/shard_map/ppermute | solution.py:26
  187.2 12.5 %collective-permute-start.3 = (f32[128,1]{0,1:T(1,128)S(1)}, f32[128,1]{0,1:T(1,128)S(1)}, u32[]{:S(2)}, u32[]{:S(2)}) collective-permute-start(f32[128,1]{0,1:T(1,128)S(1)} %collective-permute-done.1), channel_id=1, source_target_pairs={{0,2},{2,4},{4,6},{6,8},{8,10},{10,12},{12,14},{14,16},{16,18},{18... | collective-permute-start | bytes 1544 | tf_op jit(solution)/shard_map/ppermute | solution.py:21
  197.6 7.0 %collective-permute-start.4 = (f32[128,1]{0,1:T(1,128)S(1)}, f32[128,1]{0,1:T(1,128)S(1)}, u32[]{:S(2)}, u32[]{:S(2)}) collective-permute-start(f32[128,1]{0,1:T(1,128)S(1)} %collective-permute-done.2), channel_id=1, source_target_pairs={{0,30},{2,0},{4,2},{6,4},{8,6},{10,8},{12,10},{14,12},{16,14},{18,... | collective-permute-start | bytes 1544 | tf_op jit(solution)/shard_map/ppermute | solution.py:26
  199.7 7.0 %collective-permute-start.5 = (f32[128,1]{0,1:T(1,128)S(1)}, f32[128,1]{0,1:T(1,128)S(1)}, u32[]{:S(2)}, u32[]{:S(2)}) collective-permute-start(f32[128,1]{0,1:T(1,128)S(1)} %collective-permute-done.3), channel_id=1, source_target_pairs={{0,2},{2,4},{4,6},{6,8},{8,10},{10,12},{12,14},{14,16},{16,18},{18... | collective-permute-start | bytes 1544 | tf_op jit(solution)/shard_map/ppermute | solution.py:21
  204.6 5.5 %collective-permute-start.6 = (f32[128,1]{0,1:T(1,128)S(1)}, f32[128,1]{0,1:T(1,128)S(1)}, u32[]{:S(2)}, u32[]{:S(2)}) collective-permute-start(f32[128,1]{0,1:T(1,128)S(1)} %collective-permute-done.4), channel_id=1, source_target_pairs={{0,30},{2,0},{4,2},{6,4},{8,6},{10,8},{12,10},{14,12},{16,14},{18,... | collective-permute-start | bytes 1544 | tf_op jit(solution)/shard_map/ppermute | solution.py:26
  206.8 6.7 %collective-permute-start.7 = (f32[128,1]{0,1:T(1,128)S(1)}, f32[128,1]{0,1:T(1,128)S(1)}, u32[]{:S(2)}, u32[]{:S(2)}) collective-permute-start(f32[128,1]{0,1:T(1,128)S(1)} %collective-permute-done.5), channel_id=1, source_target_pairs={{0,2},{2,4},{4,6},{6,8},{8,10},{10,12},{12,14},{14,16},{16,18},{18... | collective-permute-start | bytes 1544 | tf_op jit(solution)/shard_map/ppermute | solution.py:21
  210.1 5.5 %collective-permute-start.8 = (f32[128,1]{0,1:T(1,128)S(1)}, f32[128,1]{0,1:T(1,128)S(1)}, u32[]{:S(2)}, u32[]{:S(2)}) collective-permute-start(f32[128,1]{0,1:T(1,128)S(1)} %collective-permute-done.6), channel_id=1, source_target_pairs={{0,30},{2,0},{4,2},{6,4},{8,6},{10,8},{12,10},{14,12},{16,14},{18,... | collective-permute-start | bytes 1544 | tf_op jit(solution)/shard_map/ppermute | solution.py:26
  213.5 6.7 %collective-permute-start.9 = (f32[128,1]{0,1:T(1,128)S(1)}, f32[128,1]{0,1:T(1,128)S(1)}, u32[]{:S(2)}, u32[]{:S(2)}) collective-permute-start(f32[128,1]{0,1:T(1,128)S(1)} %collective-permute-done.7), channel_id=1, source_target_pairs={{0,2},{2,4},{4,6},{6,8},{8,10},{10,12},{12,14},{14,16},{16,18},{18... | collective-permute-start | bytes 1544 | tf_op jit(solution)/shard_map/ppermute | solution.py:21
  215.6 6.5 %collective-permute-start.10 = (f32[128,1]{0,1:T(1,128)S(1)}, f32[128,1]{0,1:T(1,128)S(1)}, u32[]{:S(2)}, u32[]{:S(2)}) collective-permute-start(f32[128,1]{0,1:T(1,128)S(1)} %collective-permute-done.8), channel_id=1, source_target_pairs={{0,30},{2,0},{4,2},{6,4},{8,6},{10,8},{12,10},{14,12},{16,14},{18,... | collective-permute-start | bytes 1544 | tf_op jit(solution)/shard_map/ppermute | solution.py:26
  220.2 6.7 %collective-permute-start.11 = (f32[128,1]{0,1:T(1,128)S(1)}, f32[128,1]{0,1:T(1,128)S(1)}, u32[]{:S(2)}, u32[]{:S(2)}) collective-permute-start(f32[128,1]{0,1:T(1,128)S(1)} %collective-permute-done.9), channel_id=1, source_target_pairs={{0,2},{2,4},{4,6},{6,8},{8,10},{10,12},{12,14},{14,16},{16,18},{18... | collective-permute-start | bytes 1544 | tf_op jit(solution)/shard_map/ppermute | solution.py:21
  222.1 6.7 %collective-permute-start.12 = (f32[128,1]{0,1:T(1,128)S(1)}, f32[128,1]{0,1:T(1,128)S(1)}, u32[]{:S(2)}, u32[]{:S(2)}) collective-permute-start(f32[128,1]{0,1:T(1,128)S(1)} %collective-permute-done.10), channel_id=1, source_target_pairs={{0,30},{2,0},{4,2},{6,4},{8,6},{10,8},{12,10},{14,12},{16,14},{18,... | collective-permute-start | bytes 1544 | tf_op jit(solution)/shard_map/ppermute | solution.py:26
  226.9 6.7 %collective-permute-start.13 = (f32[128,1]{0,1:T(1,128)S(1)}, f32[128,1]{0,1:T(1,128)S(1)}, u32[]{:S(2)}, u32[]{:S(2)}) collective-permute-start(f32[128,1]{0,1:T(1,128)S(1)} %collective-permute-done.11), channel_id=1, source_target_pairs={{0,2},{2,4},{4,6},{6,8},{8,10},{10,12},{12,14},{14,16},{16,18},{18... | collective-permute-start | bytes 1544 | tf_op jit(solution)/shard_map/ppermute | solution.py:21
  228.8 6.8 %collective-permute-start.14 = (f32[128,1]{0,1:T(1,128)S(1)}, f32[128,1]{0,1:T(1,128)S(1)}, u32[]{:S(2)}, u32[]{:S(2)}) collective-permute-start(f32[128,1]{0,1:T(1,128)S(1)} %collective-permute-done.12), channel_id=1, source_target_pairs={{0,30},{2,0},{4,2},{6,4},{8,6},{10,8},{12,10},{14,12},{16,14},{18,... | collective-permute-start | bytes 1544 | tf_op jit(solution)/shard_map/ppermute | solution.py:26
  233.6 5.5 %collective-permute-start.15 = (f32[128,1]{0,1:T(1,128)S(1)}, f32[128,1]{0,1:T(1,128)S(1)}, u32[]{:S(2)}, u32[]{:S(2)}) collective-permute-start(f32[128,1]{0,1:T(1,128)S(1)} %collective-permute-done.13), channel_id=1, source_target_pairs={{0,2},{2,4},{4,6},{6,8},{8,10},{10,12},{12,14},{14,16},{16,18},{18... | collective-permute-start | bytes 1544 | tf_op jit(solution)/shard_map/ppermute | solution.py:21
  239.4 4.0 %copy-start.4 = (bf16[1,512]{1,0:T(2,128)(2,1)S(1)}, bf16[1,512]{1,0:T(2,128)(2,1)}, u32[]{:S(2)}) copy-start(bf16[1,512]{1,0:T(2,128)(2,1)} %param.13) | copy-start | bytes 3076
  239.4 5.4 %copy-start.6 = (bf16[2048,512]{1,0:T(8,128)(2,1)S(1)}, bf16[2048,512]{1,0:T(8,128)(2,1)}, u32[]{:S(2)}) copy-start(bf16[2048,512]{1,0:T(8,128)(2,1)} %all-gather.5.cloned.1.call-done) | copy-start | bytes 6291460
Sparse Core Ops, SparseCore 0:
  10.7 75.9 all-gather.6
  106.1 114.1 all-gather.4
